TPU v7x, 256 devices: a whole 4x4x8 slice. The times are simulated.
256 devices in a mesh: dp: 16 (over y_hi, z), seq: 16 (over x, y_lo, core).
Axes of the slice: x: 4, y: 4 (y_hi: 2, y_lo: 2; y = y_hi * 2 + y_lo), z: 8, core: 2. Of those that a mesh axis runs over, the one named last changes fastest.
Arguments:
- queries: bfloat16 [16, 2048, 2048], P('dp', 'seq'), may hold values from -6 to 6
- key_states: bfloat16 [16, 2048, 2048], P('dp', 'seq'), may hold values from -6 to 6
- value_states: bfloat16 [16, 2048, 2048], P('dp', 'seq'), may hold values from -6 to 6
- cotangent: bfloat16 [16, 2048, 2048], P('dp', 'seq'), may hold values from -6 to 6
- filter_taps: float32 [7, 2048], replicated, may hold values from -3 to 3
Outputs:
- conv_output: bfloat16 [16, 2048, 2048], P('dp', 'seq')
- grad_queries: bfloat16 [16, 2048, 2048], P('dp', 'seq')
- grad_keys: bfloat16 [16, 2048, 2048], P('dp', 'seq')
- grad_values: bfloat16 [16, 2048, 2048], P('dp', 'seq')
- filter_gradient: float32 [7, 2048], replicated
All inputs are finite; a program needn't handle non-finite values.
Results may differ from a plain program's by a relative error of at most 0.015.
Values may be sent and summed in bfloat16 or wider, within the bound.
No kernel may reach another device: no remote copies, remote signals or barrier semaphores. Data moves between devices by JAX's collectives and lax.ppermute only.
A program may use at most 128 MiB of HBM per device.

v0:
```python
import math
import jax
import jax.numpy as jnp
import numpy as np
from jax import lax
from jax.sharding import Mesh
from jax.sharding import PartitionSpec as P

HD = 128
TAPS = 7
GROUP_HEADS = 2
SEQ = ("sc", "core")


def padded(value, width):
    peers = lax.axis_size("sc") * lax.axis_size("core")
    length = value.shape[0]
    up = [(i, (i + 1) % peers) for i in range(peers)]
    down = [(j, i) for i, j in up]
    before = lax.ppermute(value[length - width :], SEQ, up)
    after = lax.ppermute(value[:width], SEQ, down)
    return jnp.concatenate([before, value, after], axis=0)


def to_chip_rows(value):
    rows, channels = value.shape
    split = value.reshape(rows, 2, channels // 2)
    return lax.all_to_all(split, "core", 1, 0, tiled=True).reshape(2 * rows, channels // 2)


def from_chip_rows(value):
    rows2, half = value.shape
    split = value.reshape(2, rows2 // 2, 1, half)
    out = lax.all_to_all(split, "core", 0, 2, tiled=True)
    return out.reshape(rows2 // 2, 2 * half)


def on_device(queries, key_states, value_states, cotangent, filter_taps):
    tok_rows = queries.shape[1]
    channels = queries.shape[2]
    chips = lax.axis_size("sc")
    seq_total = tok_rows * chips * 2
    chip_rows = 2 * tok_rows
    half_channels = channels // 2
    head_count = half_channels // HD
    group_width = GROUP_HEADS * HD
    group_count = head_count // GROUP_HEADS
    score_scale = HD ** (-0.5)
    half_width = (TAPS - 1) // 2
    local_q = queries[0]
    local_k = key_states[0]
    local_v = value_states[0]
    local_g = cotangent[0]
    grad_pad = padded(local_g, half_width)
    grad_sum = jnp.zeros((tok_rows, channels), jnp.float32)
    for tap_index in range(TAPS):
        start_row = 2 * half_width - tap_index
        grad_sum = grad_sum + filter_taps[tap_index] * grad_pad[
            start_row : start_row + tok_rows
        ].astype(jnp.float32)
    grad_attn = grad_sum.astype(jnp.bfloat16)
    chip_q = to_chip_rows(local_q)
    chip_k = to_chip_rows(local_k)
    chip_v = to_chip_rows(local_v)
    chip_d = to_chip_rows(grad_attn)
    chip_index = lax.axis_index("sc")
    query_pos = chip_index * chip_rows + jnp.arange(chip_rows, dtype=jnp.int32)
    key_pos = jnp.arange(seq_total, dtype=jnp.int32)
    visible = query_pos[:, None] >= key_pos[None, :]
    attended_parts, grad_q_parts, key_parts, value_parts = ([], [], [], [])
    for group_index in range(group_count):
        cols = slice(group_index * group_width, (group_index + 1) * group_width)
        k_all = lax.all_gather(chip_k[:, cols], "sc", axis=0, tiled=True)
        v_all = lax.all_gather(chip_v[:, cols], "sc", axis=0, tiled=True)
        q_part = chip_q[:, cols].reshape(chip_rows, GROUP_HEADS, HD)
        d_part = chip_d[:, cols].reshape(chip_rows, GROUP_HEADS, HD)
        k_part = k_all.reshape(seq_total, GROUP_HEADS, HD)
        v_part = v_all.reshape(seq_total, GROUP_HEADS, HD)
        scores = (
            jnp.einsum("thd,uhd->htu", q_part, k_part, preferred_element_type=jnp.float32)
            * score_scale
        )
        row_top = jnp.max(jnp.where(visible, scores, -jnp.inf), -1, keepdims=True)
        raw = jnp.where(visible, jnp.exp(scores - row_top), 0.0)
        row_total = jnp.sum(raw, -1, keepdims=True)
        probs = raw / row_total
        probs_low = probs.astype(jnp.bfloat16)
        attended = jnp.einsum("htu,uhd->thd", probs_low, v_part, preferred_element_type=jnp.float32)
        attended_parts.append(attended.astype(jnp.bfloat16).reshape(chip_rows, group_width))
        dprob = jnp.einsum("thd,uhd->htu", d_part, v_part, preferred_element_type=jnp.float32)
        row_delta = jnp.sum(probs * dprob, -1, keepdims=True)
        dscore = (probs * (dprob - row_delta) * score_scale).astype(jnp.bfloat16)
        grad_q = jnp.einsum("htu,uhd->thd", dscore, k_part, preferred_element_type=jnp.float32)
        grad_q_parts.append(grad_q.astype(jnp.bfloat16).reshape(chip_rows, group_width))
        key_term = jnp.einsum("htu,thd->uhd", dscore, q_part, preferred_element_type=jnp.float32)
        value_term = jnp.einsum(
            "htu,thd->uhd", probs_low, d_part, preferred_element_type=jnp.float32
        )
        key_parts.append(
            lax.psum_scatter(
                key_term.astype(jnp.bfloat16).reshape(seq_total, group_width),
                "sc",
                scatter_dimension=0,
                tiled=True,
            )
        )
        value_parts.append(
            lax.psum_scatter(
                value_term.astype(jnp.bfloat16).reshape(seq_total, group_width),
                "sc",
                scatter_dimension=0,
                tiled=True,
            )
        )
    attn_out = from_chip_rows(jnp.concatenate(attended_parts, axis=1))
    grad_queries = from_chip_rows(jnp.concatenate(grad_q_parts, axis=1))
    grad_keys = from_chip_rows(jnp.concatenate(key_parts, axis=1))
    grad_values = from_chip_rows(jnp.concatenate(value_parts, axis=1))
    out_pad = padded(attn_out, half_width)
    conv_sum = jnp.zeros((tok_rows, channels), jnp.float32)
    filter_rows = []
    local_gf = local_g.astype(jnp.float32)
    for tap_index in range(TAPS):
        moved = out_pad[tap_index : tap_index + tok_rows].astype(jnp.float32)
        conv_sum = conv_sum + filter_taps[tap_index] * moved
        filter_rows.append(jnp.sum(moved * local_gf, 0))
    filter_gradient = lax.psum(jnp.stack(filter_rows, 0), ("dp", "sc", "core"))
    conv_output = conv_sum.astype(jnp.bfloat16)
    return (
        conv_output[None],
        grad_queries[None],
        grad_keys[None],
        grad_values[None],
        filter_gradient,
    )


def solution(mesh):
    devices = np.asarray(mesh.devices)
    dp_size, seq_size = devices.shape
    split_mesh = Mesh(devices.reshape(dp_size, seq_size // 2, 2), ("dp", "sc", "core"))
    block = P("dp", SEQ, None)
    in_specs = (block, block, block, block, P())
    out_specs = (block, block, block, block, P())
    return jax.shard_map(
        on_device, mesh=split_mesh, in_specs=in_specs, out_specs=out_specs, check_vma=False
    )
```

profile of v0, /device:TPU:1, one launch (start us, length us, event | category | flops | bytes accessed | tf_op | source)
XLA Modules:
  0.0 740.7 jit_solution(332086236696625652)
XLA Ops:
  36.2 20.8 %collective-permute-done.2 = bf16[3,2048]{0,1:T(8,128)(2,1)S(1)} collective-permute-done((bf16[3,2048]{0,1:T(8,128)(2,1)}, bf16[3,2048]{0,1:T(8,128)(2,1)S(1)}, u32[]{:S(2)}, u32[]{:S(2)}) %collective-permute-start.2) | collective-permute-done | bytes 12320 | tf_op jit(solution)/shard_map/ppermute | solution.py:21
  71.0 34.5 %all-gather.15.cloned.1.call-done = bf16[2048,256]{1,0:T(8,128)(2,1)} async-done(((bf16[256,256]{1,0:T(8,128)(2,1)}), bf16[2048,256]{1,0:T(8,128)(2,1)}) %all-gather.15.cloned.1.call-update) | async-done | bytes 1048592 | tf_op jit(solution)/shard_map/all_gather | solution.py:74
  116.5 9.7 %convolution_convert_fusion.2 = bf16[2,2048,128]{1,2,0:T(8,128)(2,1)} fusion(bf16[256,2,128]{0,2,1:T(8,128)(2,1)} %bitcast.232, f32[2,256,2048]{2,1,0:T(8,128)} %fusion.183, f32[2,256,2048]{2,1,0:T(8,128)} %get-tuple-element.66, f32[2,256]{1,0:T(2,128)} %get-tuple-element.65), kind=kOutput, calls=%fused_computation.45 | convolution fusion | flops 276302336 | bytes 9570304 | tf_op jit(solution)/shard_map/htu,thd->uhd/dot_general | solution.py:95
  127.9 19.7 %all-gather.17.cloned.1.call-done = bf16[2048,256]{1,0:T(8,128)(2,1)} async-done(((bf16[256,256]{1,0:T(8,128)(2,1)}), bf16[2048,256]{1,0:T(8,128)(2,1)}) %all-gather.17.cloned.1.call-update) | async-done | bytes 1048592 | tf_op jit(solution)/shard_map/all_gather | solution.py:73
  149.9 41.5 %all-gather.19.cloned.1.call-done = bf16[2048,256]{1,0:T(8,128)(2,1)} async-done(((bf16[256,256]{1,0:T(8,128)(2,1)}), bf16[2048,256]{1,0:T(8,128)(2,1)}) %all-gather.19.cloned.1.call-update) | async-done | bytes 1048592 | tf_op jit(solution)/shard_map/all_gather | solution.py:74
  203.1 9.7 %convolution_convert_fusion.1 = bf16[2,2048,128]{1,2,0:T(8,128)(2,1)} fusion(bf16[256,2,128]{0,2,1:T(8,128)(2,1)} %bitcast.236, f32[2,256,2048]{2,1,0:T(8,128)} %fusion.184, f32[2,256,2048]{2,1,0:T(8,128)} %get-tuple-element.64, f32[2,256]{1,0:T(2,128)} %get-tuple-element.63), kind=kOutput, calls=%fused_computation.44 | convolution fusion | flops 276302336 | bytes 9570304 | tf_op jit(solution)/shard_map/htu,thd->uhd/dot_general | solution.py:95
  214.6 19.3 %all-gather.21.cloned.1.call-done = bf16[2048,256]{1,0:T(8,128)(2,1)} async-done(((bf16[256,256]{1,0:T(8,128)(2,1)}), bf16[2048,256]{1,0:T(8,128)(2,1)}) %all-gather.21.cloned.1.call-update) | async-done | bytes 1048592 | tf_op jit(solution)/shard_map/all_gather | solution.py:73
  236.1 41.4 %all-gather.23.cloned.1.call-done = bf16[2048,256]{1,0:T(8,128)(2,1)} async-done(((bf16[256,256]{1,0:T(8,128)(2,1)}), bf16[2048,256]{1,0:T(8,128)(2,1)}) %all-gather.23.cloned.1.call-update) | async-done | bytes 1048592 | tf_op jit(solution)/shard_map/all_gather | solution.py:74
  290.2 9.7 %convolution_convert_fusion = bf16[2,2048,128]{1,2,0:T(8,128)(2,1)} fusion(bf16[256,2,128]{0,2,1:T(8,128)(2,1)} %bitcast.238, f32[2,256,2048]{2,1,0:T(8,128)} %fusion.185, f32[2,256,2048]{2,1,0:T(8,128)} %get-tuple-element.62, f32[2,256]{1,0:T(2,128)} %get-tuple-element.61), kind=kOutput, calls=%fused_computation.43 | convolution fusion | flops 276302336 | bytes 9570304 | tf_op jit(solution)/shard_map/htu,thd->uhd/dot_general | solution.py:95
  301.1 18.5 %all-gather.9.cloned.1.call-done = bf16[2048,256]{1,0:T(8,128)(2,1)} async-done(((bf16[256,256]{1,0:T(8,128)(2,1)}), bf16[2048,256]{1,0:T(8,128)(2,1)}) %all-gather.9.cloned.1.call-update) | async-done | bytes 1048592 | tf_op jit(solution)/shard_map/all_gather | solution.py:73
  321.9 42.0 %all-gather.11.cloned.1.call-done = bf16[2048,256]{1,0:T(8,128)(2,1)} async-done(((bf16[256,256]{1,0:T(8,128)(2,1)}), bf16[2048,256]{1,0:T(8,128)(2,1)}) %all-gather.11.cloned.1.call-update) | async-done | bytes 1048592 | tf_op jit(solution)/shard_map/all_gather | solution.py:74
  376.0 9.6 %convolution_convert_fusion.3 = bf16[2,2048,128]{1,2,0:T(8,128)(2,1)} fusion(bf16[256,2,128]{0,2,1:T(8,128)(2,1)S(1)} %bitcast.234, f32[2,256,2048]{2,1,0:T(8,128)} %fusion.182, f32[2,256,2048]{2,1,0:T(8,128)} %get-tuple-element.68, f32[2,256]{1,0:T(2,128)S(1)} %get-tuple-element.67), kind=kOutput, calls=%fused_computation.46 | convolution fusion | flops 276302336 | bytes 9570304 | tf_op jit(solution)/shard_map/htu,thd->uhd/dot_general | solution.py:95
  396.6 8.2 %fusion.91 = bf16[256,2,128]{2,0,1:T(8,128)(2,1)S(1)} fusion(bf16[2048,2,128]{0,2,1:T(8,128)(2,1)} %bitcast.215, f32[2,256,2048]{2,1,0:T(8,128)} %fusion.183, f32[2,256,2048]{2,1,0:T(8,128)} %get-tuple-element.66, f32[2,256]{1,0:T(2,128)S(1)} %copy-done.23), kind=kOutput, calls=%fused_computation.111 | convolution fusion | flops 275843584 | bytes 9570304 | tf_op jit(solution)/shard_map/htu,uhd->thd/dot_general | solution.py:93
  412.7 7.9 %fusion.94 = bf16[256,2,128]{2,0,1:T(8,128)(2,1)S(1)} fusion(bf16[2048,2,128]{0,2,1:T(8,128)(2,1)S(1)} %bitcast.217, f32[2,256,2048]{2,1,0:T(8,128)} %fusion.184, f32[2,256,2048]{2,1,0:T(8,128)} %get-tuple-element.64, f32[2,256]{1,0:T(2,128)S(1)} %copy-done.24), kind=kOutput, calls=%fused_computation.112 | convolution fusion | flops 275843584 | bytes 9570304 | tf_op jit(solution)/shard_map/htu,uhd->thd/dot_general | solution.py:93
  429.3 8.1 %fusion.97 = bf16[256,2,128]{2,0,1:T(8,128)(2,1)S(1)} fusion(bf16[2048,2,128]{0,2,1:T(8,128)(2,1)S(1)} %bitcast.219, f32[2,256,2048]{2,1,0:T(8,128)} %fusion.185, f32[2,256,2048]{2,1,0:T(8,128)} %get-tuple-element.62, f32[2,256]{1,0:T(2,128)} %get-tuple-element.61), kind=kOutput, calls=%fused_computation.113 | convolution fusion | flops 275843584 | bytes 9570304 | tf_op jit(solution)/shard_map/htu,uhd->thd/dot_general | solution.py:93
  437.9 8.0 %fusion.88 = bf16[256,2,128]{2,0,1:T(8,128)(2,1)S(1)} fusion(bf16[2048,2,128]{0,2,1:T(8,128)(2,1)S(1)} %bitcast.221, f32[2,256,2048]{2,1,0:T(8,128)} %fusion.182, f32[2,256,2048]{2,1,0:T(8,128)} %get-tuple-element.68, f32[2,256]{1,0:T(2,128)} %copy-done.26), kind=kOutput, calls=%fused_computation.110 | convolution fusion | flops 275843584 | bytes 9570304 | tf_op jit(solution)/shard_map/htu,uhd->thd/dot_general | solution.py:93
  447.1 8.7 %all-to-all-start.3 = ((bf16[2,128,1,1024]{3,1,2,0:T(8,128)(2,1)}), bf16[2,128,1,1024]{3,1,2,0:T(8,128)(2,1)S(1)}, u32[]{:S(2)}, u32[]{:S(2)}) async-start(bf16[2,128,1,1024]{3,1,2,0:T(8,128)(2,1)} %maximum_bitcast_fusion), calls=%async_computation.3 | async-start | bytes 1048576 | tf_op jit(solution)/shard_map/all_to_all | solution.py:34
  464.4 7.4 collective-permute-done.1
  480.0 81.5 %psum.7 = f32[7,2048]{1,0:T(8,128)} all-reduce(f32[7,2048]{1,0:T(8,128)S(1)} %stack.31), channel_id=1, replica_groups=mesh['dp'=16,'sc'=8,'core'=2] {'dp','sc','core'}, use_global_device_ids=true, to_apply=%region_27.28 | all-reduce | flops 14336 | bytes 114688 | tf_op jit(solution)/shard_map/psum | solution.py:127
  563.0 23.9 %reduce-scatter.19.cloned.1.call-done = bf16[256,256]{0,1:T(8,128)(2,1)} async-done(((bf16[2048,256]{0,1:T(8,128)(2,1)}), bf16[256,256]{0,1:T(8,128)(2,1)}) %reduce-scatter.19.cloned.1.call-update) | async-done | bytes 131088 | tf_op jit(solution)/shard_map/reduce_scatter | solution.py:108
  586.8 43.3 %reduce-scatter.21.cloned.1.call-done = bf16[256,256]{0,1:T(8,128)(2,1)} async-done(((bf16[2048,256]{0,1:T(8,128)(2,1)}), bf16[256,256]{0,1:T(8,128)(2,1)}) %reduce-scatter.21.cloned.1.call-update) | async-done | bytes 131088 | tf_op jit(solution)/shard_map/reduce_scatter | solution.py:108
  630.1 43.4 %reduce-scatter.23.cloned.1.call-done = bf16[256,256]{0,1:T(8,128)(2,1)} async-done(((bf16[2048,256]{0,1:T(8,128)(2,1)}), bf16[256,256]{0,1:T(8,128)(2,1)}) %reduce-scatter.23.cloned.1.call-update) | async-done | bytes 131088 | tf_op jit(solution)/shard_map/reduce_scatter | solution.py:108
  673.5 43.4 %reduce-scatter.17.cloned.1.call-done = bf16[256,256]{0,1:T(8,128)(2,1)} async-done(((bf16[2048,256]{0,1:T(8,128)(2,1)}), bf16[256,256]{0,1:T(8,128)(2,1)}) %reduce-scatter.17.cloned.1.call-update) | async-done | bytes 131088 | tf_op jit(solution)/shard_map/reduce_scatter | solution.py:108
  718.3 9.0 %all_to_all.123 = bf16[2,128,1,1024]{3,1,2,0:T(8,128)(2,1)S(1)} all-to-all(bf16[2,128,1,1024]{3,1,2,0:T(8,128)(2,1)S(1)} %bitcast.199), channel_id=1, replica_groups=mesh['dp'=16,'sc'=8,'core'=2] {'core'}, dimensions={0} | all-to-all | bytes 1048576 | tf_op jit(solution)/shard_map/all_to_all | solution.py:34
  (195 shorter events, 156.8 us)
Async XLA Ops:
  7.2 62.3 %all-gather.13.cloned.1.call-start = ((), (), s32[]{:S(2)}) async-start(), calls=%async_computation.18 | async-start | bytes 1179648 | tf_op jit(solution)/shard_map/all_gather | solution.py:73
  16.8 88.7 %all-gather.15.cloned.1.call-start = ((), (), s32[]{:S(2)}) async-start(), calls=%async_computation.19 | async-start | bytes 1179648 | tf_op jit(solution)/shard_map/all_gather | solution.py:74
  22.4 125.3 %all-gather.17.cloned.1.call-start = ((), (), s32[]{:S(2)}) async-start(), calls=%async_computation.20 | async-start | bytes 1179648 | tf_op jit(solution)/shard_map/all_gather | solution.py:73
  23.1 168.3 %all-gather.19.cloned.1.call-start = ((), (), s32[]{:S(2)}) async-start(), calls=%async_computation.21 | async-start | bytes 1179648 | tf_op jit(solution)/shard_map/all_gather | solution.py:74
  23.7 210.2 %all-gather.21.cloned.1.call-start = ((), (), s32[]{:S(2)}) async-start(), calls=%async_computation.22 | async-start | bytes 1179648 | tf_op jit(solution)/shard_map/all_gather | solution.py:73
  24.3 253.2 %all-gather.23.cloned.1.call-start = ((), (), s32[]{:S(2)}) async-start(), calls=%async_computation.23 | async-start | bytes 1179648 | tf_op jit(solution)/shard_map/all_gather | solution.py:74
  24.8 294.7 %all-gather.9.cloned.1.call-start = ((), (), s32[]{:S(2)}) async-start(), calls=%async_computation.16 | async-start | bytes 1179648 | tf_op jit(solution)/shard_map/all_gather | solution.py:73
  26.6 8.0 %all-to-all-start = ((bf16[128,2,1024]{0,2,1:T(8,128)(2,1)}), bf16[128,2,1024]{0,2,1:T(8,128)(2,1)S(1)}, u32[]{:S(2)}, u32[]{:S(2)}) async-start(bf16[128,2,1024]{0,2,1:T(8,128)(2,1)} %bitcast.1), calls=%async_computation | async-start | bytes 1048576 | tf_op jit(solution)/shard_map/all_to_all | solution.py:28
  30.5 333.4 %all-gather.11.cloned.1.call-start = ((), (), s32[]{:S(2)}) async-start(), calls=%async_computation.17 | async-start | bytes 1179648 | tf_op jit(solution)/shard_map/all_gather | solution.py:74
  31.7 25.3 %collective-permute-start.2 = (bf16[3,2048]{0,1:T(8,128)(2,1)}, bf16[3,2048]{0,1:T(8,128)(2,1)S(1)}, u32[]{:S(2)}, u32[]{:S(2)}) collective-permute-start(bf16[3,2048]{0,1:T(8,128)(2,1)} %get-tuple-element.38), channel_id=1, source_target_pairs={{1,0},{2,1},{3,2},{4,3},{5,4},{6,5},{7,6},{8,7},{9,8},{10,9},{11,1... | collective-permute-start | bytes 36872 | tf_op jit(solution)/shard_map/ppermute | solution.py:21
  31.8 26.3 %collective-permute-start.3 = (bf16[3,2048]{0,1:T(8,128)(2,1)S(1)}, bf16[3,2048]{0,1:T(8,128)(2,1)}, u32[]{:S(2)}, u32[]{:S(2)}) collective-permute-start(bf16[3,2048]{0,1:T(8,128)(2,1)S(1)} %get-tuple-element.39), channel_id=1, source_target_pairs={{0,1},{1,2},{2,3},{3,4},{4,5},{5,6},{6,7},{7,8},{8,9},{9,10},{10,1... | collective-permute-start | bytes 36872 | tf_op jit(solution)/shard_map/ppermute | solution.py:20
  33.5 528.1 %reduce-scatter.11.cloned.1.call-start = ((), (), s32[]{:S(2)}) async-start(), calls=%async_computation.25 | async-start | bytes 1179648 | tf_op jit(solution)/shard_map/reduce_scatter | solution.py:100
  126.1 435.4 %reduce-scatter.13.cloned.1.call-start = ((), (), s32[]{:S(2)}) async-start(), calls=%async_computation.26 | async-start | bytes 1179648 | tf_op jit(solution)/shard_map/reduce_scatter | solution.py:100
  212.8 348.8 %reduce-scatter.15.cloned.1.call-start = ((), (), s32[]{:S(2)}) async-start(), calls=%async_computation.27 | async-start | bytes 1179648 | tf_op jit(solution)/shard_map/reduce_scatter | solution.py:100
  300.0 261.6 %reduce-scatter.9.cloned.1.call-start = ((), (), s32[]{:S(2)}) async-start(), calls=%async_computation.24 | async-start | bytes 1179648 | tf_op jit(solution)/shard_map/reduce_scatter | solution.py:100
  301.1 68.9 %copy-start.13 = (bf16[256,256]{0,1:T(8,128)(2,1)}, bf16[256,256]{0,1:T(8,128)(2,1)S(1)}, u32[]{:S(2)}) copy-start(bf16[256,256]{0,1:T(8,128)(2,1)S(1)} %copy.319) | copy-start | bytes 393220
  385.7 201.1 %reduce-scatter.19.cloned.1.call-start = ((), (), s32[]{:S(2)}) async-start(), calls=%async_computation.29 | async-start | bytes 1179648 | tf_op jit(solution)/shard_map/reduce_scatter | solution.py:108
  389.5 240.6 %reduce-scatter.21.cloned.1.call-start = ((), (), s32[]{:S(2)}) async-start(), calls=%async_computation.30 | async-start | bytes 1179648 | tf_op jit(solution)/shard_map/reduce_scatter | solution.py:108
  393.4 280.1 %reduce-scatter.23.cloned.1.call-start = ((), (), s32[]{:S(2)}) async-start(), calls=%async_computation.31 | async-start | bytes 1179648 | tf_op jit(solution)/shard_map/reduce_scatter | solution.py:108
  412.2 304.7 %reduce-scatter.17.cloned.1.call-start = ((), (), s32[]{:S(2)}) async-start(), calls=%async_computation.28 | async-start | bytes 1179648 | tf_op jit(solution)/shard_map/reduce_scatter | solution.py:108
  447.1 10.0 %all-to-all-start.3 = ((bf16[2,128,1,1024]{3,1,2,0:T(8,128)(2,1)}), bf16[2,128,1,1024]{3,1,2,0:T(8,128)(2,1)S(1)}, u32[]{:S(2)}, u32[]{:S(2)}) async-start(bf16[2,128,1,1024]{3,1,2,0:T(8,128)(2,1)} %maximum_bitcast_fusion), calls=%async_computation.3 | async-start | bytes 1048576 | tf_op jit(solution)/shard_map/all_to_all | solution.py:34
  457.1 5.6 all-to-all-start.5
  461.7 2.4 collective-permute-start
  461.7 10.0 %collective-permute-start.1 = (bf16[3,2048]{0,1:T(8,128)(2,1)S(1)}, bf16[3,2048]{0,1:T(8,128)(2,1)S(1)}, u32[]{:S(2)}, u32[]{:S(2)}) collective-permute-start(bf16[3,2048]{0,1:T(8,128)(2,1)S(1)} %bitcast.222), channel_id=1, source_target_pairs={{1,0},{2,1},{3,2},{4,3},{5,4},{6,5},{7,6},{8,7},{9,8},{10,9},{11,1... | collective-permute-start | bytes 36872 | tf_op jit(solution)/shard_map/ppermute | solution.py:21
  (27 other events, 320.9 us)
Sparse Core Ops, SparseCore 0:
  16.9 45.7 all-gather.12
  64.6 40.9 all-gather.14
  107.3 40.2 all-gather.16
  149.3 42.1 all-gather.18
  193.0 40.7 all-gather.20
  236.1 41.3 all-gather.22
  279.3 40.2 all-gather.8
  321.9 41.8 all-gather.10
  366.4 41.0 reduce-scatter.10
  409.8 41.1 reduce-scatter.12
  453.5 44.8 reduce-scatter.14
  500.8 42.3 reduce-scatter.8
  545.8 41.0 reduce-scatter.18
  589.2 40.8 reduce-scatter.20
  632.5 40.9 reduce-scatter.22
  675.9 40.9 reduce-scatter.16
where the time goes:
time: 750 us; the launch traced here: 741 us
  waiting for transfers between devices  404 us (54%)
  matrix products  136 us (18%)
  blocking collectives  110 us (15%)
  local copies, waits for them, and re-layouts  38.6 us (5%)
  starting transfers between devices  20.2 us (3%)
  other arithmetic  17.8 us (2%)
  between operations  14.8 us (2%)
    all_gather x4, waiting for transfers between devices, on_device(): v_all = lax.all_gather(chip_v[:, cols], 'sc', axis=0, tiled=True)  159 us
    reduce_scatter x4, waiting for transfers between devices, on_device(): lax.psum_scatter(value_term.astype(jnp.bfloat16).reshape(seq_total, group...  154 us
    psum x1, blocking collectives, on_device(): filter_gradient = lax.psum(jnp.stack(filter_rows, 0), ('dp', 'sc', 'core'))  81.5 us
    all_gather x4, waiting for transfers between devices, on_device(): k_all = lax.all_gather(chip_k[:, cols], 'sc', axis=0, tiled=True)  57.5 us
    dot_general x4, matrix products, on_device(): jnp.einsum('htu,thd->uhd', dscore, q_part, preferred_element_type=jnp.flo...  38.7 us
    dot_general x4, matrix products, on_device(): jnp.einsum('htu,uhd->thd', dscore, k_part, preferred_element_type=jnp.flo...  32.2 us
    ppermute x2, waiting for transfers between devices, padded(): after = lax.ppermute(value[:width], SEQ, down)  28.2 us
    sub x4, matrix products, on_device(): raw = jnp.where(visible, jnp.exp(scores - row_top), 0.0)  24.9 us
  transfers between devices with their start and end apart: 23, of which 15 were waited for; matrix products, arithmetic and copies ran while one was open for 25% of the time, Pallas kernels for 0%

commit v1 on v0

--- a/solution.py
+++ b/solution.py
@@ -10,6 +10,12 @@
 TAPS = 7
 GROUP_HEADS = 2
 SEQ = ("sc", "core")
+
+
+def trade_parts(x, axis, split, join):
+    shards = jnp.split(x, lax.axis_size(axis), axis=split)
+    received = lax.all_to_all(jnp.stack(shards), axis, 0, 0)
+    return jnp.concatenate(received, axis=join)
 
 
 def padded(value, width):
@@ -25,7 +31,7 @@
 def to_chip_rows(value):
     rows, channels = value.shape
     split = value.reshape(rows, 2, channels // 2)
-    return lax.all_to_all(split, "core", 1, 0, tiled=True).reshape(2 * rows, channels // 2)
+    return trade_parts(split, "core", 1, 0).reshape(2 * rows, channels // 2)
 
 
 def from_chip_rows(value):

time: 750 us -> 748 us (level)
    ppermute x2, waiting for transfers between devices: 1.06 us -> 16 us  [padded(): before = lax.ppermute(value[length - width:], SEQ, up)]
    reduce_scatter x4, waiting for transfers between devices: 154 us -> 143 us  [on_device(): lax.psum_scatter(value_term.astype(jnp.bfloat16).reshape(seq_total, group...]
  transfers between devices with their start and end apart: 23 -> 23, of which waited for: 15 -> 16; matrix products, arithmetic and copies ran while one was open for 25% -> 25% of each run, Pallas kernels for 0% -> 0%
where the time goes in v1:
time: 748 us; the launch traced here: 739 us
  waiting for transfers between devices  405 us (54%)
  matrix products  135 us (18%)
  blocking collectives  105 us (14%)
  local copies, waits for them, and re-layouts  34.1 us (5%)
  other arithmetic  23.2 us (3%)
  starting transfers between devices  20.4 us (3%)
  between operations  15.2 us (2%)
    all_gather x4, waiting for transfers between devices, on_device(): v_all = lax.all_gather(chip_v[:, cols], 'sc', axis=0, tiled=True)  156 us
    reduce_scatter x4, waiting for transfers between devices, on_device(): lax.psum_scatter(value_term.astype(jnp.bfloat16).reshape(seq_total, group...  143 us
    psum x1, blocking collectives, on_device(): filter_gradient = lax.psum(jnp.stack(filter_rows, 0), ('dp', 'sc', 'core'))  77 us
    all_gather x4, waiting for transfers between devices, on_device(): k_all = lax.all_gather(chip_k[:, cols], 'sc', axis=0, tiled=True)  60.9 us
    dot_general x4, matrix products, on_device(): jnp.einsum('htu,thd->uhd', dscore, q_part, preferred_element_type=jnp.flo...  38.7 us
    dot_general x4, matrix products, on_device(): jnp.einsum('htu,uhd->thd', dscore, k_part, preferred_element_type=jnp.flo...  32.6 us
    sub x4, matrix products, on_device(): raw = jnp.where(visible, jnp.exp(scores - row_top), 0.0)  26.2 us
    ppermute x2, waiting for transfers between devices, padded(): after = lax.ppermute(value[:width], SEQ, down)  25.9 us
  transfers between devices with their start and end apart: 23, of which 16 were waited for; matrix products, arithmetic and copies ran while one was open for 25% of the time, Pallas kernels for 0%

profile of v1, /device:TPU:1, one launch (start us, length us, event | category | flops | bytes accessed | tf_op | source)
XLA Modules:
  0.0 738.6 jit_solution(14710767202516883610)
XLA Ops:
  37.4 20.8 %collective-permute-done.2 = bf16[3,2048]{0,1:T(8,128)(2,1)S(1)} collective-permute-done((bf16[3,2048]{0,1:T(8,128)(2,1)}, bf16[3,2048]{0,1:T(8,128)(2,1)S(1)}, u32[]{:S(2)}, u32[]{:S(2)}) %collective-permute-start.2) | collective-permute-done | bytes 12320 | tf_op jit(solution)/shard_map/ppermute | solution.py:27
  72.2 32.7 %all-gather.13.cloned.1.call-done = bf16[2048,256]{1,0:T(8,128)(2,1)} async-done(((bf16[256,256]{1,0:T(8,128)(2,1)}), bf16[2048,256]{1,0:T(8,128)(2,1)}) %all-gather.13.cloned.1.call-update) | async-done | bytes 1048592 | tf_op jit(solution)/shard_map/all_gather | solution.py:80
  116.2 9.7 %convolution_convert_fusion.6 = bf16[2,128,2048]{2,1,0:T(8,128)(2,1)} fusion(bf16[256,2,128]{0,2,1:T(8,128)(2,1)} %bitcast.242, f32[2,256,2048]{2,1,0:T(8,128)} %fusion.182, f32[2,256,2048]{2,1,0:T(8,128)} %get-tuple-element.74, f32[2,256]{1,0:T(2,128)} %get-tuple-element.73), kind=kOutput, calls=%fused_computation.49 | convolution fusion | flops 276302336 | bytes 9570304 | tf_op jit(solution)/shard_map/htu,thd->uhd/dot_general | solution.py:101
  127.7 20.1 %all-gather.19.cloned.1.call-done = bf16[2048,256]{1,0:T(8,128)(2,1)} async-done(((bf16[256,256]{1,0:T(8,128)(2,1)}), bf16[2048,256]{1,0:T(8,128)(2,1)}) %all-gather.19.cloned.1.call-update) | async-done | bytes 1048592 | tf_op jit(solution)/shard_map/all_gather | solution.py:79
  150.1 40.8 %all-gather.17.cloned.1.call-done = bf16[2048,256]{1,0:T(8,128)(2,1)} async-done(((bf16[256,256]{1,0:T(8,128)(2,1)}), bf16[2048,256]{1,0:T(8,128)(2,1)}) %all-gather.17.cloned.1.call-update) | async-done | bytes 1048592 | tf_op jit(solution)/shard_map/all_gather | solution.py:80
  202.9 9.7 %convolution_convert_fusion.5 = bf16[2,128,2048]{2,1,0:T(8,128)(2,1)} fusion(bf16[256,2,128]{0,2,1:T(8,128)(2,1)} %bitcast.246, f32[2,256,2048]{2,1,0:T(8,128)} %fusion.183, f32[2,256,2048]{2,1,0:T(8,128)} %get-tuple-element.72, f32[2,256]{1,0:T(2,128)} %get-tuple-element.71), kind=kOutput, calls=%fused_computation.48 | convolution fusion | flops 276302336 | bytes 9570304 | tf_op jit(solution)/shard_map/htu,thd->uhd/dot_general | solution.py:101
  213.6 19.9 %all-gather.23.cloned.1.call-done = bf16[2048,256]{1,0:T(8,128)(2,1)} async-done(((bf16[256,256]{1,0:T(8,128)(2,1)}), bf16[2048,256]{1,0:T(8,128)(2,1)}) %all-gather.23.cloned.1.call-update) | async-done | bytes 1048592 | tf_op jit(solution)/shard_map/all_gather | solution.py:79
  235.7 40.9 %all-gather.21.cloned.1.call-done = bf16[2048,256]{1,0:T(8,128)(2,1)} async-done(((bf16[256,256]{1,0:T(8,128)(2,1)}), bf16[2048,256]{1,0:T(8,128)(2,1)}) %all-gather.21.cloned.1.call-update) | async-done | bytes 1048592 | tf_op jit(solution)/shard_map/all_gather | solution.py:80
  287.8 9.7 %convolution_convert_fusion.4 = bf16[2,128,2048]{2,1,0:T(8,128)(2,1)} fusion(bf16[256,2,128]{0,2,1:T(8,128)(2,1)} %bitcast.248, f32[2,256,2048]{2,1,0:T(8,128)} %fusion.184, f32[2,256,2048]{2,1,0:T(8,128)} %get-tuple-element.70, f32[2,256]{1,0:T(2,128)} %get-tuple-element.69), kind=kOutput, calls=%fused_computation.47 | convolution fusion | flops 276302336 | bytes 9570304 | tf_op jit(solution)/shard_map/htu,thd->uhd/dot_general | solution.py:101
  298.6 20.9 %all-gather.11.cloned.1.call-done = bf16[2048,256]{1,0:T(8,128)(2,1)} async-done(((bf16[256,256]{1,0:T(8,128)(2,1)}), bf16[2048,256]{1,0:T(8,128)(2,1)}) %all-gather.11.cloned.1.call-update) | async-done | bytes 1048592 | tf_op jit(solution)/shard_map/all_gather | solution.py:79
  321.8 41.3 %all-gather.9.cloned.1.call-done = bf16[2048,256]{1,0:T(8,128)(2,1)} async-done(((bf16[256,256]{1,0:T(8,128)(2,1)}), bf16[2048,256]{1,0:T(8,128)(2,1)}) %all-gather.9.cloned.1.call-update) | async-done | bytes 1048592 | tf_op jit(solution)/shard_map/all_gather | solution.py:80
  373.5 9.6 %convolution_convert_fusion.7 = bf16[2,128,2048]{2,1,0:T(8,128)(2,1)} fusion(bf16[256,2,128]{0,2,1:T(8,128)(2,1)S(1)} %bitcast.244, f32[2,256,2048]{2,1,0:T(8,128)} %fusion.181, f32[2,256,2048]{2,1,0:T(8,128)} %get-tuple-element.76, f32[2,256]{1,0:T(2,128)S(1)} %get-tuple-element.75), kind=kOutput, calls=%fused_computation.50 | convolution fusion | flops 276302336 | bytes 9570304 | tf_op jit(solution)/shard_map/htu,thd->uhd/dot_general | solution.py:101
  394.2 8.3 %fusion.91 = bf16[256,2,128]{0,2,1:T(8,128)(2,1)S(1)} fusion(bf16[2048,2,128]{0,2,1:T(8,128)(2,1)} %bitcast.225, f32[2,256,2048]{2,1,0:T(8,128)} %fusion.182, f32[2,256,2048]{2,1,0:T(8,128)} %get-tuple-element.74, f32[2,256]{1,0:T(2,128)S(1)} %copy-done.27), kind=kOutput, calls=%fused_computation.111 | convolution fusion | flops 275843584 | bytes 9570304 | tf_op jit(solution)/shard_map/htu,uhd->thd/dot_general | solution.py:99
  409.9 8.1 %fusion.94 = bf16[256,2,128]{0,2,1:T(8,128)(2,1)S(1)} fusion(bf16[2048,2,128]{0,2,1:T(8,128)(2,1)} %bitcast.228, f32[2,256,2048]{2,1,0:T(8,128)} %fusion.183, f32[2,256,2048]{2,1,0:T(8,128)} %get-tuple-element.72, f32[2,256]{1,0:T(2,128)S(1)} %copy-done.28), kind=kOutput, calls=%fused_computation.112 | convolution fusion | flops 275843584 | bytes 9570304 | tf_op jit(solution)/shard_map/htu,uhd->thd/dot_general | solution.py:99
  426.5 7.9 %fusion.97 = bf16[256,2,128]{0,2,1:T(8,128)(2,1)S(1)} fusion(bf16[2048,2,128]{0,2,1:T(8,128)(2,1)S(1)} %bitcast.230, f32[2,256,2048]{2,1,0:T(8,128)} %fusion.184, f32[2,256,2048]{2,1,0:T(8,128)} %get-tuple-element.70, f32[2,256]{1,0:T(2,128)} %get-tuple-element.69), kind=kOutput, calls=%fused_computation.113 | convolution fusion | flops 275843584 | bytes 9570304 | tf_op jit(solution)/shard_map/htu,uhd->thd/dot_general | solution.py:99
  434.5 8.3 %fusion.88 = bf16[256,2,128]{0,2,1:T(8,128)(2,1)S(1)} fusion(bf16[2048,2,128]{0,2,1:T(8,128)(2,1)} %bitcast.232, f32[2,256,2048]{2,1,0:T(8,128)} %fusion.181, f32[2,256,2048]{2,1,0:T(8,128)} %get-tuple-element.76, f32[2,256]{1,0:T(2,128)} %copy-done.31), kind=kOutput, calls=%fused_computation.110 | convolution fusion | flops 275843584 | bytes 9570304 | tf_op jit(solution)/shard_map/htu,uhd->thd/dot_general | solution.py:99
  443.7 9.0 %all-to-all-start.3 = ((bf16[2,128,1,1024]{1,3,2,0:T(8,128)(2,1)}), bf16[2,128,1,1024]{1,3,2,0:T(8,128)(2,1)S(1)}, u32[]{:S(2)}, u32[]{:S(2)}) async-start(bf16[2,128,1,1024]{1,3,2,0:T(8,128)(2,1)} %pad_maximum_fusion.7), calls=%async_computation.3 | async-start | bytes 1048576 | tf_op jit(solution)/shard_map/all_to_all | solution.py:40
  461.2 15.0 %collective-permute-done = bf16[3,2048]{0,1:T(8,128)(2,1)S(1)} collective-permute-done((bf16[3,2048]{0,1:T(8,128)(2,1)}, bf16[3,2048]{0,1:T(8,128)(2,1)S(1)}, u32[]{:S(2)}, u32[]{:S(2)}) %collective-permute-start) | collective-permute-done | bytes 12320 | tf_op jit(solution)/shard_map/ppermute | solution.py:26
  493.4 77.0 %psum.7 = f32[7,2048]{1,0:T(8,128)} all-reduce(f32[7,2048]{1,0:T(8,128)S(1)} %stack.79), channel_id=1, replica_groups=mesh['dp'=16,'sc'=8,'core'=2] {'dp','sc','core'}, use_global_device_ids=true, to_apply=%region_27.28 | all-reduce | flops 14336 | bytes 114688 | tf_op jit(solution)/shard_map/psum | solution.py:133
  571.8 12.2 %reduce-scatter.19.cloned.1.call-done = bf16[256,256]{0,1:T(8,128)(2,1)} async-done(((bf16[2048,256]{0,1:T(8,128)(2,1)}), bf16[256,256]{0,1:T(8,128)(2,1)}) %reduce-scatter.19.cloned.1.call-update) | async-done | bytes 131088 | tf_op jit(solution)/shard_map/reduce_scatter | solution.py:114
  584.0 43.8 %reduce-scatter.21.cloned.1.call-done = bf16[256,256]{0,1:T(8,128)(2,1)} async-done(((bf16[2048,256]{0,1:T(8,128)(2,1)}), bf16[256,256]{0,1:T(8,128)(2,1)}) %reduce-scatter.21.cloned.1.call-update) | async-done | bytes 131088 | tf_op jit(solution)/shard_map/reduce_scatter | solution.py:114
  627.8 43.4 %reduce-scatter.23.cloned.1.call-done = bf16[256,256]{0,1:T(8,128)(2,1)} async-done(((bf16[2048,256]{0,1:T(8,128)(2,1)}), bf16[256,256]{0,1:T(8,128)(2,1)}) %reduce-scatter.23.cloned.1.call-update) | async-done | bytes 131088 | tf_op jit(solution)/shard_map/reduce_scatter | solution.py:114
  671.2 43.4 %reduce-scatter.17.cloned.1.call-done = bf16[256,256]{0,1:T(8,128)(2,1)} async-done(((bf16[2048,256]{0,1:T(8,128)(2,1)}), bf16[256,256]{0,1:T(8,128)(2,1)}) %reduce-scatter.17.cloned.1.call-update) | async-done | bytes 131088 | tf_op jit(solution)/shard_map/reduce_scatter | solution.py:114
  715.9 8.9 %all_to_all.83 = bf16[2,128,1,1024]{3,1,2,0:T(8,128)(2,1)S(1)} all-to-all(bf16[2,128,1,1024]{3,1,2,0:T(8,128)(2,1)S(1)} %bitcast.213), channel_id=1, replica_groups=mesh['dp'=16,'sc'=8,'core'=2] {'core'}, dimensions={0} | all-to-all | bytes 1048576 | tf_op jit(solution)/shard_map/all_to_all | solution.py:40
  (210 shorter events, 162.0 us)
Async XLA Ops:
  7.2 63.5 %all-gather.15.cloned.1.call-start = ((), (), s32[]{:S(2)}) async-start(), calls=%async_computation.19 | async-start | bytes 1179648 | tf_op jit(solution)/shard_map/all_gather | solution.py:79
  16.8 88.1 %all-gather.13.cloned.1.call-start = ((), (), s32[]{:S(2)}) async-start(), calls=%async_computation.18 | async-start | bytes 1179648 | tf_op jit(solution)/shard_map/all_gather | solution.py:80
  22.6 125.2 %all-gather.19.cloned.1.call-start = ((), (), s32[]{:S(2)}) async-start(), calls=%async_computation.21 | async-start | bytes 1179648 | tf_op jit(solution)/shard_map/all_gather | solution.py:79
  23.3 167.5 %all-gather.17.cloned.1.call-start = ((), (), s32[]{:S(2)}) async-start(), calls=%async_computation.20 | async-start | bytes 1179648 | tf_op jit(solution)/shard_map/all_gather | solution.py:80
  23.9 209.6 %all-gather.23.cloned.1.call-start = ((), (), s32[]{:S(2)}) async-start(), calls=%async_computation.23 | async-start | bytes 1179648 | tf_op jit(solution)/shard_map/all_gather | solution.py:79
  24.5 252.1 %all-gather.21.cloned.1.call-start = ((), (), s32[]{:S(2)}) async-start(), calls=%async_computation.22 | async-start | bytes 1179648 | tf_op jit(solution)/shard_map/all_gather | solution.py:80
  25.1 294.4 %all-gather.11.cloned.1.call-start = ((), (), s32[]{:S(2)}) async-start(), calls=%async_computation.17 | async-start | bytes 1179648 | tf_op jit(solution)/shard_map/all_gather | solution.py:79
  27.0 8.8 %all-to-all-start.1 = ((bf16[2,128,1,1024]{1,3,2,0:T(8,128)(2,1)}), bf16[2,128,1,1024]{1,3,2,0:T(8,128)(2,1)S(1)}, u32[]{:S(2)}, u32[]{:S(2)}) async-start(bf16[2,128,1,1024]{1,3,2,0:T(8,128)(2,1)} %pad_maximum_fusion.5), calls=%async_computation.1 | async-start | bytes 1048576 | tf_op jit(solution)/shard_map/all_to_all | solution.py:17
  30.8 332.2 %all-gather.9.cloned.1.call-start = ((), (), s32[]{:S(2)}) async-start(), calls=%async_computation.16 | async-start | bytes 1179648 | tf_op jit(solution)/shard_map/all_gather | solution.py:80
  32.1 26.1 %collective-permute-start.2 = (bf16[3,2048]{0,1:T(8,128)(2,1)}, bf16[3,2048]{0,1:T(8,128)(2,1)S(1)}, u32[]{:S(2)}, u32[]{:S(2)}) collective-permute-start(bf16[3,2048]{0,1:T(8,128)(2,1)} %get-tuple-element.40), channel_id=1, source_target_pairs={{1,0},{2,1},{3,2},{4,3},{5,4},{6,5},{7,6},{8,7},{9,8},{10,9},{11,1... | collective-permute-start | bytes 36872 | tf_op jit(solution)/shard_map/ppermute | solution.py:27
  32.2 27.0 %collective-permute-start.3 = (bf16[3,2048]{0,1:T(8,128)(2,1)S(1)}, bf16[3,2048]{0,1:T(8,128)(2,1)}, u32[]{:S(2)}, u32[]{:S(2)}) collective-permute-start(bf16[3,2048]{0,1:T(8,128)(2,1)S(1)} %get-tuple-element.41), channel_id=1, source_target_pairs={{0,1},{1,2},{2,3},{3,4},{4,5},{5,6},{6,7},{7,8},{8,9},{9,10},{10,1... | collective-permute-start | bytes 36872 | tf_op jit(solution)/shard_map/ppermute | solution.py:26
  33.9 536.5 %reduce-scatter.11.cloned.1.call-start = ((), (), s32[]{:S(2)}) async-start(), calls=%async_computation.25 | async-start | bytes 1179648 | tf_op jit(solution)/shard_map/reduce_scatter | solution.py:106
  125.9 444.5 %reduce-scatter.13.cloned.1.call-start = ((), (), s32[]{:S(2)}) async-start(), calls=%async_computation.26 | async-start | bytes 1179648 | tf_op jit(solution)/shard_map/reduce_scatter | solution.py:106
  212.6 357.8 %reduce-scatter.15.cloned.1.call-start = ((), (), s32[]{:S(2)}) async-start(), calls=%async_computation.27 | async-start | bytes 1179648 | tf_op jit(solution)/shard_map/reduce_scatter | solution.py:106
  297.5 272.9 %reduce-scatter.9.cloned.1.call-start = ((), (), s32[]{:S(2)}) async-start(), calls=%async_computation.24 | async-start | bytes 1179648 | tf_op jit(solution)/shard_map/reduce_scatter | solution.py:106
  298.6 68.6 %copy-start.16 = (bf16[256,256]{0,1:T(8,128)(2,1)}, bf16[256,256]{0,1:T(8,128)(2,1)S(1)}, u32[]{:S(2)}) copy-start(bf16[256,256]{0,1:T(8,128)(2,1)S(1)} %copy.279) | copy-start | bytes 393220
  383.2 200.8 %reduce-scatter.19.cloned.1.call-start = ((), (), s32[]{:S(2)}) async-start(), calls=%async_computation.29 | async-start | bytes 1179648 | tf_op jit(solution)/shard_map/reduce_scatter | solution.py:114
  386.9 240.8 %reduce-scatter.21.cloned.1.call-start = ((), (), s32[]{:S(2)}) async-start(), calls=%async_computation.30 | async-start | bytes 1179648 | tf_op jit(solution)/shard_map/reduce_scatter | solution.py:114
  391.0 280.2 %reduce-scatter.23.cloned.1.call-start = ((), (), s32[]{:S(2)}) async-start(), calls=%async_computation.31 | async-start | bytes 1179648 | tf_op jit(solution)/shard_map/reduce_scatter | solution.py:114
  409.6 305.0 %reduce-scatter.17.cloned.1.call-start = ((), (), s32[]{:S(2)}) async-start(), calls=%async_computation.28 | async-start | bytes 1179648 | tf_op jit(solution)/shard_map/reduce_scatter | solution.py:114
  443.7 10.3 %all-to-all-start.3 = ((bf16[2,128,1,1024]{1,3,2,0:T(8,128)(2,1)}), bf16[2,128,1,1024]{1,3,2,0:T(8,128)(2,1)S(1)}, u32[]{:S(2)}, u32[]{:S(2)}) async-start(bf16[2,128,1,1024]{1,3,2,0:T(8,128)(2,1)} %pad_maximum_fusion.7), calls=%async_computation.3 | async-start | bytes 1048576 | tf_op jit(solution)/shard_map/all_to_all | solution.py:40
  454.0 6.1 all-to-all-start.5
  459.0 17.2 %collective-permute-start = (bf16[3,2048]{0,1:T(8,128)(2,1)}, bf16[3,2048]{0,1:T(8,128)(2,1)S(1)}, u32[]{:S(2)}, u32[]{:S(2)}) collective-permute-start(bf16[3,2048]{0,1:T(8,128)(2,1)} %bitcast.31), channel_id=1, source_target_pairs={{0,1},{1,2},{2,3},{3,4},{4,5},{5,6},{6,7},{7,8},{8,9},{9,10},{10,1... | collective-permute-start | bytes 36872 | tf_op jit(solution)/shard_map/ppermute | solution.py:26
  459.0 22.4 %collective-permute-start.1 = (bf16[3,2048]{0,1:T(8,128)(2,1)}, bf16[3,2048]{0,1:T(8,128)(2,1)}, u32[]{:S(2)}, u32[]{:S(2)}) collective-permute-start(bf16[3,2048]{0,1:T(8,128)(2,1)} %bitcast.39), channel_id=1, source_target_pairs={{1,0},{2,1},{3,2},{4,3},{5,4},{6,5},{7,6},{8,7},{9,8},{10,9},{11,1... | collective-permute-start | bytes 36872 | tf_op jit(solution)/shard_map/ppermute | solution.py:27
  (32 other events, 468.0 us)
Sparse Core Ops, SparseCore 0:
  16.9 46.0 all-gather.14
  64.8 40.0 all-gather.12
  106.7 41.0 all-gather.18
  149.4 41.3 all-gather.16
  192.5 40.9 all-gather.22
  235.1 41.4 all-gather.20
  278.4 41.0 all-gather.10
  321.9 41.1 all-gather.8
  365.6 41.2 reduce-scatter.10
  409.2 41.2 reduce-scatter.12
  453.0 42.6 reduce-scatter.14
  498.1 42.3 reduce-scatter.8
  543.0 40.8 reduce-scatter.18
  586.4 41.3 reduce-scatter.20
  630.1 40.9 reduce-scatter.22
  673.6 40.9 reduce-scatter.16
